TPU v7x, 32 devices: a whole 2x2x4 slice. The times are simulated.
32 devices in a mesh: groups: 2 (over y), cam: 4 (over z), tm: 2 (over x), chan: 2 (over core).
Axes of the slice: x: 2, y: 2, z: 4, core: 2. Of those that a mesh axis runs over, the one named last changes fastest.
Arguments:
- video: bfloat16 [16, 8, 16, 8, 256], P(('groups', 'cam'), 'tm', None, None, 'chan'), parts along dimension 0, may hold values from -6 to 6
- conv_weight: bfloat16 [27, 256, 256], P(None, None, 'chan'), may hold values from -0.078125 to 0.078125
- proj_weight: bfloat16 [256, 16], P('chan'), may hold values from -0.375 to 0.375
- rig_sizes: int32 [8], P('groups'), parts along dimension 0, may hold values from 1 to 3, as said below
- camera_order: int32 [16], P('groups'), parts along dimension 0, may hold values from 0 to 7, as said below
- owner_slot: int32 [8], P('groups'), parts along dimension 0, may hold values from 0 to 3, as said below
- cotangent: bfloat16 [8, 8, 16, 128], P(('groups', 'cam'), 'tm'), parts along dimension 0, may hold values from -6 to 6
Outputs:
- robot_latent: float32 [8, 8, 16, 128], P(('groups', 'cam'), 'tm'), parts along dimension 0
- grad_conv: bfloat16 [54, 256, 256], P('groups', None, 'chan'), parts along dimension 0
- grad_proj: float32 [512, 16], P(('groups', 'chan')), parts along dimension 0
- grad_video: bfloat16 [16, 8, 16, 8, 256], P(('groups', 'cam'), 'tm', None, None, 'chan'), parts along dimension 0
There are 2 independent parts, one for each index of `groups`. A program takes and returns all parts, laid end to end along the dimension named above; an argument that names none is the same for every part. Nothing has to cross between parts.
Inputs may be any that keep to these rules, and one draw needn't show every extreme that they name: `rig_sizes`: the sizes sum to 8; the largest is exactly 3. `camera_order`: A permutation; the cameras whose places fall from rig_sizes[0] + ... + rig_sizes[r-1] to below rig_sizes[0] + ... + rig_sizes[r] belong to robot r. `owner_slot`: A permutation of the output rows.
All inputs are finite; a program needn't handle non-finite values.
Results may differ from a plain program's by a relative error of at most 0.0059.
Values may be sent and summed in bfloat16 or wider, within the bound.
No kernel may reach another device: no remote copies, remote signals or barrier semaphores. Data moves between devices by JAX's collectives and lax.ppermute only.
A program may use at most 128 MiB of HBM per device.

v0:
```python
import jax
import jax.numpy as jnp
from jax import lax
from jax.sharding import PartitionSpec as P

KT = 3
KS = 3


def shifted(shard, axis, by):
    size = lax.axis_size(axis)
    pairs = [(i, i + by) for i in range(size) if 0 <= i + by < size]
    return lax.ppermute(shard, axis, pairs)


def tap_offsets():
    return [
        (shift_t, shift_h, shift_w)
        for shift_t in range(KT)
        for shift_h in range(KS)
        for shift_w in range(KS)
    ]


def forward_taps(extended, weight, frames, height, width):
    channels = extended.shape[-1]
    summed = jnp.zeros((extended.shape[0] * frames * height * width, weight.shape[2]), jnp.float32)
    for tap_index, (shift_t, shift_h, shift_w) in enumerate(tap_offsets()):
        window = extended[
            :, shift_t : shift_t + frames, shift_h : shift_h + height, shift_w : shift_w + width, :
        ].reshape(-1, channels)
        summed = summed + jnp.dot(window, weight[tap_index], preferred_element_type=jnp.float32)
    return summed


def weight_taps(extended, grad_rows, frames, height, width):
    channels = extended.shape[-1]
    results = []
    for shift_t, shift_h, shift_w in tap_offsets():
        window = extended[
            :, shift_t : shift_t + frames, shift_h : shift_h + height, shift_w : shift_w + width, :
        ].reshape(-1, channels)
        results.append(
            lax.dot_general(
                window, grad_rows, (((0,), (0,)), ((), ())), preferred_element_type=jnp.float32
            )
        )
    return jnp.stack(results)


def input_taps(grad_rows, weight, batch, frames, height, width):
    channels = weight.shape[1]
    pad_half = KS // 2
    padded = jnp.zeros(
        (batch, frames + KT - 1, height + KS - 1, width + KS - 1, channels), jnp.float32
    )
    for tap_index, (shift_t, shift_h, shift_w) in enumerate(tap_offsets()):
        backed = lax.dot_general(
            grad_rows,
            weight[tap_index],
            (((1,), (1,)), ((), ())),
            preferred_element_type=jnp.float32,
        )
        padded = padded.at[
            :, shift_t : shift_t + frames, shift_h : shift_h + height, shift_w : shift_w + width, :
        ].add(backed.reshape(batch, frames, height, width, channels))
    return padded[:, :, pad_half : pad_half + height, pad_half : pad_half + width, :]


def joining_matrix(rig_sizes, camera_order, owner_slot):
    robots = rig_sizes.shape[0]
    ends = jnp.cumsum(rig_sizes)
    robot_of = jnp.sum((ends[None, :] <= camera_order[:, None]).astype(jnp.int32), axis=1)
    member = robot_of[:, None] == jnp.arange(robots, dtype=jnp.int32)[None, :]
    slot_of = jnp.sum(jnp.where(member, owner_slot[None, :], 0), axis=1)
    count_of = jnp.sum(jnp.where(member, rig_sizes[None, :], 0), axis=1)
    share = 1.0 / count_of.astype(jnp.float32)
    placed = slot_of[None, :] == jnp.arange(robots, dtype=jnp.int32)[:, None]
    return jnp.where(placed, share[None, :], jnp.zeros_like(share)[None, :])


def body(video, conv_weight, proj_weight, rig_sizes, camera_order, owner_slot, cotangent):
    cam_dev, frames, height, width, half_chan = video.shape
    pad_half = KS // 2
    lat_width = proj_weight.shape[1]
    cache_half = shifted(video[:, frames - (KT - 1) :], "tm", 1)
    whole_now, whole_cache = (
        lax.all_gather(video, "chan", axis=4, tiled=True),
        lax.all_gather(cache_half, "chan", axis=4, tiled=True),
    )
    extended = jnp.concatenate([whole_cache, whole_now], axis=1)
    extended = jnp.pad(
        extended, ((0, 0), (0, 0), (pad_half, pad_half), (pad_half, pad_half), (0, 0))
    )
    pre = forward_taps(extended, conv_weight, frames, height, width)
    sigma = jax.nn.sigmoid(pre)
    act = (pre * sigma).astype(jnp.bfloat16)
    latent_part = jnp.dot(act, proj_weight, preferred_element_type=jnp.float32)
    latent = lax.psum(latent_part, "chan").astype(jnp.bfloat16)
    mixing = joining_matrix(rig_sizes, camera_order, owner_slot)
    cam_index = lax.axis_index("cam")
    my_row = lax.dynamic_slice_in_dim(mixing, cam_index, 1, 0)
    latent_maps = latent.reshape(cam_dev, frames, height, width * lat_width)
    block_in = lax.all_gather(latent_maps, "cam", axis=0, tiled=True)
    count_in = block_in.shape[0]
    flat_in = block_in.reshape(count_in, -1).astype(jnp.float32)
    added = jnp.dot(
        my_row, flat_in, precision=lax.Precision.HIGHEST, preferred_element_type=jnp.float32
    )
    robot_latent = added.reshape(
        jnp.zeros((1, frames, height, width * lat_width), jnp.float32).shape
    )
    my_cols = lax.dynamic_slice_in_dim(mixing, cam_index * cam_dev, cam_dev, 1)
    block_in = lax.all_gather(cotangent, "cam", axis=0, tiled=True)
    count_in = block_in.shape[0]
    flat_in = block_in.reshape(count_in, -1).astype(jnp.float32)
    spread = lax.dot_general(
        my_cols,
        flat_in,
        (((0,), (0,)), ((), ())),
        precision=lax.Precision.HIGHEST,
        preferred_element_type=jnp.float32,
    )
    dlatent = spread.astype(jnp.bfloat16).reshape(-1, lat_width)
    grad_proj_local = lax.dot_general(
        act, dlatent, (((0,), (0,)), ((), ())), preferred_element_type=jnp.float32
    )
    dact = lax.dot_general(
        dlatent, proj_weight, (((1,), (1,)), ((), ())), preferred_element_type=jnp.float32
    )
    dpre = (dact * sigma * (1.0 + pre * (1.0 - sigma))).astype(jnp.bfloat16)
    full_back = input_taps(dpre, conv_weight, cam_dev, frames, height, width)
    cache_part = full_back[:, : KT - 1]
    incoming = shifted(cache_part, "tm", -1)
    own_part = full_back[:, KT - 1 :]
    own_part = own_part.at[:, frames - (KT - 1) :].add(incoming)
    grad_conv_local = weight_taps(extended, dpre, frames, height, width)
    grad_conv, grad_proj = lax.psum((grad_conv_local, grad_proj_local), ("cam", "tm"))
    grad_video = lax.psum_scatter(
        own_part.astype(jnp.bfloat16), "chan", scatter_dimension=4, tiled=True
    )
    return (robot_latent, grad_conv.astype(jnp.bfloat16), grad_proj, grad_video)


def solution(mesh):
    return jax.shard_map(
        body,
        mesh=mesh,
        in_specs=(
            P(("groups", "cam"), "tm", None, None, "chan"),
            P(None, None, "chan"),
            P("chan", None),
            P("groups"),
            P("groups"),
            P("groups"),
            P(("groups", "cam"), "tm", None, None),
        ),
        out_specs=(
            P(("groups", "cam"), "tm", None, None),
            P("groups", None, "chan"),
            P(("groups", "chan"), None),
            P(("groups", "cam"), "tm", None, None, "chan"),
        ),
        check_vma=False,
    )
```

profile of v0, /device:TPU:0, one launch (start us, length us, event | category | flops | bytes accessed | tf_op | source)
XLA Modules:
  0.0 450.1 jit_solution(12302339504369722204)
XLA Ops:
  8.2 4.8 %collective-permute-start = (bf16[2,2,16,8,128]{4,3,2,1,0:T(8,128)(2,1)S(1)}, bf16[2,2,16,8,128]{4,3,2,1,0:T(8,128)(2,1)S(1)}, u32[]{:S(2)}, u32[]{:S(2)}) collective-permute-start(bf16[2,2,16,8,128]{4,3,2,1,0:T(8,128)(2,1)S(1)} %slice.1486), channel_id=1, source_target_pairs={{0,2},{1,3},{4,6},{5,7},{8,10},{9,11},{12,14},{13,15},{16,18},{17,... | collective-permute-start | bytes 393224 | tf_op jit(solution)/shard_map/ppermute | solution.py:13
  15.4 13.6 %all_gather.15 = bf16[4,4,16,128]{3,2,1,0:T(8,128)(2,1)S(1)} all-gather(bf16[1,4,16,128]{3,2,1,0:T(8,128)(2,1)} %param.69), channel_id=1, replica_groups=mesh['groups'=2,'cam'=4,'tm'=2,'chan'=2] {'cam'}, dimensions={0}, use_global_device_ids=true | all-gather | bytes 81920 | tf_op jit(solution)/shard_map/all_gather | solution.py:114
  60.3 6.7 %scatter-add.95 = f32[2,6,18,10,256]{4,3,2,1,0:T(8,128)} dynamic-update-slice(f32[2,6,18,10,256]{4,3,2,1,0:T(8,128)} %scatter-add.94, f32[2,4,16,8,256]{4,3,2,1,0:T(8,128)S(1)} %convolution_add_fusion.25, s32[]{:T(128)} %constant.917.clone.1, s32[]{:T(128)} %constant.917.clone.1, s32[]{:T(128)} %constant.917.clone.1, s32[]{:T(128)} %constant.926.clone.1, s32[]{:T(128)} %constant.917.clone.1) | dynamic-update-slice | bytes 2097156 | tf_op jit(solution)/shard_map/scatter-add | solution.py:66
  68.9 6.7 %scatter-add.96 = f32[2,6,18,10,256]{4,3,2,1,0:T(8,128)} dynamic-update-slice(f32[2,6,18,10,256]{4,3,2,1,0:T(8,128)} %scatter-add.95, f32[2,4,16,8,256]{4,3,2,1,0:T(8,128)S(1)} %convolution_add_fusion.24, s32[]{:T(128)} %constant.917.clone.1, s32[]{:T(128)} %constant.917.clone.1, s32[]{:T(128)} %constant.917.clone.1, s32[]{:T(128)} %constant.924.clone.1, s32[]{:T(128)} %constant.917.clone.1) | dynamic-update-slice | bytes 2097156 | tf_op jit(solution)/shard_map/scatter-add | solution.py:66
  80.0 6.7 %scatter-add.100 = f32[2,6,18,10,256]{4,3,2,1,0:T(8,128)} dynamic-update-slice(f32[2,6,18,10,256]{4,3,2,1,0:T(8,128)} %fusion.7, f32[2,4,16,8,256]{4,3,2,1,0:T(8,128)S(1)} %convolution_add_fusion.22, s32[]{:T(128)} %constant.917.clone.1, s32[]{:T(128)} %constant.917.clone.1, s32[]{:T(128)} %constant.926.clone.1, s32[]{:T(128)} %constant.926.clone.1, s32[]{:T(128)} %constant.917.clone.1) | dynamic-update-slice | bytes 2097156 | tf_op jit(solution)/shard_map/scatter-add | solution.py:66
  86.7 3.8 convolution_add_fusion.21
  90.5 8.6 %scatter-add.101 = f32[2,6,18,10,256]{4,3,2,1,0:T(8,128)} dynamic-update-slice(f32[2,6,18,10,256]{4,3,2,1,0:T(8,128)} %scatter-add.100, f32[2,4,16,8,256]{4,3,2,1,0:T(8,128)S(1)} %convolution_add_fusion.21, s32[]{:T(128)} %constant.917.clone.1, s32[]{:T(128)} %bitcast.103, s32[]{:T(128)} %bitcast.104, s32[]{:T(128)} %bitcast.105, s32[]{:T(128)} %constant.917.clone.1) | dynamic-update-slice | bytes 2097156 | tf_op jit(solution)/shard_map/scatter-add | solution.py:66
  99.1 2.6 fusion.6
  103.6 6.7 %scatter-add.105 = f32[2,6,18,10,256]{4,3,2,1,0:T(8,128)} dynamic-update-slice(f32[2,6,18,10,256]{4,3,2,1,0:T(8,128)} %fusion.6, f32[2,4,16,8,256]{4,3,2,1,0:T(8,128)S(1)} %convolution_add_fusion.19, s32[]{:T(128)} %constant.917.clone.1, s32[]{:T(128)} %constant.917.clone.1, s32[]{:T(128)} %constant.924.clone.1, s32[]{:T(128)} %constant.926.clone.1, s32[]{:T(128)} %constant.917.clone.1) | dynamic-update-slice | bytes 2097156 | tf_op jit(solution)/shard_map/scatter-add | solution.py:66
  112.2 6.7 %scatter-add.106 = f32[2,6,18,10,256]{4,3,2,1,0:T(8,128)} dynamic-update-slice(f32[2,6,18,10,256]{4,3,2,1,0:T(8,128)} %scatter-add.105, f32[2,4,16,8,256]{4,3,2,1,0:T(8,128)S(1)} %convolution_add_fusion.18, s32[]{:T(128)} %constant.917.clone.1, s32[]{:T(128)} %constant.917.clone.1, s32[]{:T(128)} %constant.924.clone.1, s32[]{:T(128)} %constant.924.clone.1, s32[]{:T(128)} %constant.917.clone.1) | dynamic-update-slice | bytes 2097156 | tf_op jit(solution)/shard_map/scatter-add | solution.py:66
  118.9 2.7 fusion.5
  123.4 6.8 %scatter-add.110 = f32[2,6,18,10,256]{4,3,2,1,0:T(8,128)} dynamic-update-slice(f32[2,6,18,10,256]{4,3,2,1,0:T(8,128)} %fusion.5, f32[2,4,16,8,256]{4,3,2,1,0:T(8,128)S(1)} %convolution_add_fusion.16, s32[]{:T(128)} %constant.917.clone.1, s32[]{:T(128)} %constant.926.clone.1, s32[]{:T(128)} %constant.917.clone.1, s32[]{:T(128)} %constant.926.clone.1, s32[]{:T(128)} %constant.917.clone.1) | dynamic-update-slice | bytes 2097156 | tf_op jit(solution)/shard_map/scatter-add | solution.py:66
  132.1 6.8 %scatter-add.111 = f32[2,6,18,10,256]{4,3,2,1,0:T(8,128)} dynamic-update-slice(f32[2,6,18,10,256]{4,3,2,1,0:T(8,128)} %scatter-add.110, f32[2,4,16,8,256]{4,3,2,1,0:T(8,128)S(1)} %convolution_add_fusion.15, s32[]{:T(128)} %constant.917.clone.1, s32[]{:T(128)} %constant.926.clone.1, s32[]{:T(128)} %constant.917.clone.1, s32[]{:T(128)} %constant.924.clone.1, s32[]{:T(128)} %constant.917.clone.1) | dynamic-update-slice | bytes 2097156 | tf_op jit(solution)/shard_map/scatter-add | solution.py:66
  138.9 2.7 fusion.4
  143.4 6.7 %scatter-add.115 = f32[2,6,18,10,256]{4,3,2,1,0:T(8,128)} dynamic-update-slice(f32[2,6,18,10,256]{4,3,2,1,0:T(8,128)} %fusion.4, f32[2,4,16,8,256]{4,3,2,1,0:T(8,128)S(1)} %convolution_add_fusion.13, s32[]{:T(128)} %constant.917.clone.1, s32[]{:T(128)} %constant.926.clone.1, s32[]{:T(128)} %constant.926.clone.1, s32[]{:T(128)} %constant.926.clone.1, s32[]{:T(128)} %constant.917.clone.1) | dynamic-update-slice | bytes 2097156 | tf_op jit(solution)/shard_map/scatter-add | solution.py:66
  152.0 6.7 %scatter-add.116 = f32[2,6,18,10,256]{4,3,2,1,0:T(8,128)} dynamic-update-slice(f32[2,6,18,10,256]{4,3,2,1,0:T(8,128)} %scatter-add.115, f32[2,4,16,8,256]{4,3,2,1,0:T(8,128)S(1)} %convolution_add_fusion.12, s32[]{:T(128)} %constant.917.clone.1, s32[]{:T(128)} %constant.926.clone.1, s32[]{:T(128)} %constant.926.clone.1, s32[]{:T(128)} %constant.924.clone.1, s32[]{:T(128)} %constant.917.clone.1) | dynamic-update-slice | bytes 2097156 | tf_op jit(solution)/shard_map/scatter-add | solution.py:66
  158.8 2.7 fusion.3
  163.3 6.7 %scatter-add.120 = f32[2,6,18,10,256]{4,3,2,1,0:T(8,128)} dynamic-update-slice(f32[2,6,18,10,256]{4,3,2,1,0:T(8,128)} %fusion.3, f32[2,4,16,8,256]{4,3,2,1,0:T(8,128)S(1)} %convolution_add_fusion.10, s32[]{:T(128)} %constant.917.clone.1, s32[]{:T(128)} %constant.926.clone.1, s32[]{:T(128)} %constant.924.clone.1, s32[]{:T(128)} %constant.926.clone.1, s32[]{:T(128)} %constant.917.clone.1) | dynamic-update-slice | bytes 2097156 | tf_op jit(solution)/shard_map/scatter-add | solution.py:66
  172.0 6.7 %scatter-add.121 = f32[2,6,18,10,256]{4,3,2,1,0:T(8,128)} dynamic-update-slice(f32[2,6,18,10,256]{4,3,2,1,0:T(8,128)} %scatter-add.120, f32[2,4,16,8,256]{4,3,2,1,0:T(8,128)S(1)} %convolution_add_fusion.9, s32[]{:T(128)} %constant.917.clone.1, s32[]{:T(128)} %constant.926.clone.1, s32[]{:T(128)} %constant.924.clone.1, s32[]{:T(128)} %constant.924.clone.1, s32[]{:T(128)} %constant.917.clone.1) | dynamic-update-slice | bytes 2097156 | tf_op jit(solution)/shard_map/scatter-add | solution.py:66
  183.2 6.7 %scatter-add.125 = f32[2,6,18,10,256]{4,3,2,1,0:T(8,128)} dynamic-update-slice(f32[2,6,18,10,256]{4,3,2,1,0:T(8,128)} %fusion.2, f32[2,4,16,8,256]{4,3,2,1,0:T(8,128)S(1)} %convolution_add_fusion.7, s32[]{:T(128)} %constant.917.clone.1, s32[]{:T(128)} %constant.924.clone.1, s32[]{:T(128)} %constant.917.clone.1, s32[]{:T(128)} %constant.926.clone.1, s32[]{:T(128)} %constant.917.clone.1) | dynamic-update-slice | bytes 2097156 | tf_op jit(solution)/shard_map/scatter-add | solution.py:66
  191.8 6.7 %scatter-add.126 = f32[2,6,18,10,256]{4,3,2,1,0:T(8,128)} dynamic-update-slice(f32[2,6,18,10,256]{4,3,2,1,0:T(8,128)} %scatter-add.125, f32[2,4,16,8,256]{4,3,2,1,0:T(8,128)S(1)} %convolution_add_fusion.6, s32[]{:T(128)} %constant.917.clone.1, s32[]{:T(128)} %constant.924.clone.1, s32[]{:T(128)} %constant.917.clone.1, s32[]{:T(128)} %constant.924.clone.1, s32[]{:T(128)} %constant.917.clone.1) | dynamic-update-slice | bytes 2097156 | tf_op jit(solution)/shard_map/scatter-add | solution.py:66
  203.0 7.0 %scatter-add.130 = f32[2,6,18,10,256]{4,3,2,1,0:T(8,128)} dynamic-update-slice(f32[2,6,18,10,256]{4,3,2,1,0:T(8,128)} %fusion.1, f32[2,4,16,8,256]{4,3,2,1,0:T(8,128)S(1)} %convolution_add_fusion.4, s32[]{:T(128)} %constant.917.clone.1, s32[]{:T(128)} %constant.924.clone.1, s32[]{:T(128)} %constant.926.clone.1, s32[]{:T(128)} %constant.926.clone.1, s32[]{:T(128)} %constant.917.clone.1) | dynamic-update-slice | bytes 2097156 | tf_op jit(solution)/shard_map/scatter-add | solution.py:66
  211.9 6.7 %scatter-add.131 = f32[2,6,18,10,256]{4,3,2,1,0:T(8,128)} dynamic-update-slice(f32[2,6,18,10,256]{4,3,2,1,0:T(8,128)} %scatter-add.130, f32[2,4,16,8,256]{4,3,2,1,0:T(8,128)S(1)} %convolution_add_fusion.3, s32[]{:T(128)} %constant.917.clone.1, s32[]{:T(128)} %constant.924.clone.1, s32[]{:T(128)} %constant.926.clone.1, s32[]{:T(128)} %constant.924.clone.1, s32[]{:T(128)} %constant.917.clone.1) | dynamic-update-slice | bytes 2097156 | tf_op jit(solution)/shard_map/scatter-add | solution.py:66
  223.1 6.7 %scatter-add.135 = f32[2,6,18,10,256]{4,3,2,1,0:T(8,128)} dynamic-update-slice(f32[2,6,18,10,256]{4,3,2,1,0:T(8,128)} %fusion, f32[2,4,16,8,256]{4,3,2,1,0:T(8,128)S(1)} %convolution_add_fusion.1, s32[]{:T(128)} %constant.917.clone.1, s32[]{:T(128)} %constant.924.clone.1, s32[]{:T(128)} %constant.924.clone.1, s32[]{:T(128)} %constant.926.clone.1, s32[]{:T(128)} %constant.917.clone.1) | dynamic-update-slice | bytes 2097156 | tf_op jit(solution)/shard_map/scatter-add | solution.py:66
  231.7 6.7 %scatter-add.136 = f32[2,6,18,10,256]{4,3,2,1,0:T(8,128)} dynamic-update-slice(f32[2,6,18,10,256]{4,3,2,1,0:T(8,128)} %scatter-add.135, f32[2,4,16,8,256]{4,3,2,1,0:T(8,128)S(1)} %convolution_add_fusion, s32[]{:T(128)} %constant.917.clone.1, s32[]{:T(128)} %constant.924.clone.1, s32[]{:T(128)} %constant.924.clone.1, s32[]{:T(128)} %constant.924.clone.1, s32[]{:T(128)} %constant.917.clone.1) | dynamic-update-slice | bytes 2097156 | tf_op jit(solution)/shard_map/scatter-add | solution.py:66
  240.9 3.6 psum.21
  246.6 13.4 %all_gather.14 = bf16[8,4,16,128]{3,2,1,0:T(8,128)(2,1)S(1)} all-gather(bf16[2,4,16,128]{3,2,1,0:T(8,128)(2,1)S(1)} %reshape.1490), channel_id=1, replica_groups=mesh['groups'=2,'cam'=4,'tm'=2,'chan'=2] {'cam'}, dimensions={0}, use_global_device_ids=true | all-gather | bytes 163840 | tf_op jit(solution)/shard_map/all_gather | solution.py:104
  262.5 11.8 %copy.48 = bf16[2,4,16,8,256]{3,2,1,0,4:T(8,128)(2,1)} copy(bf16[2,4,16,8,256]{4,3,2,1,0:T(8,128)(2,1)S(1)} %fusion.37) | data formatting | bytes 1048576
  274.3 13.6 %reshape.1527 = bf16[256,1024]{1,0:T(8,128)(2,1)} reshape(bf16[256,2,4,16,8]{4,3,2,1,0:T(8,128)(2,1)} %bitcast.557) | data formatting | bytes 1048576
  288.0 142.3 %all-reduce.4 = (bf16[27,256,128]{2,1,0:T(8,128)(2,1)}, f32[128,16]{0,1:T(8,128)}) all-reduce(f32[27,256,128]{2,1,0:T(8,128)S(1)} %copy-done.4, f32[128,16]{0,1:T(8,128)S(1)} %fusion.156), channel_id=1, replica_groups=mesh['groups'=2,'cam'=4,'tm'=2,'chan'=2] {'cam','tm'}, use_global_device_ids=true, to_apply=%region_5.6 | all-reduce | flops 886784 | bytes 5324800 | tf_op jit(solution)/shard_map/psum | solution.py:138
  430.3 6.8 %reshape.1528 = bf16[128,2,4,16,8]{4,3,2,1,0:T(8,128)(2,1)} reshape(bf16[128,1024]{1,0:T(8,128)(2,1)} %reduce-scatter.4.cloned.1.call-done) | data formatting | bytes 524288
  437.2 6.1 %copy.49 = bf16[2,4,16,8,128]{4,3,2,1,0:T(8,128)(2,1)} copy(bf16[2,4,16,8,128]{3,2,1,0,4:T(8,128)(2,1)} %bitcast.558) | data formatting | bytes 524288
  (123 shorter events, 82.0 us)
Async XLA Ops:
  7.2 38.4 %copy-start = (bf16[128,16]{0,1:T(8,128)(2,1)S(1)}, bf16[128,16]{0,1:T(8,128)(2,1)}, u32[]{:S(2)}) copy-start(bf16[128,16]{0,1:T(8,128)(2,1)} %param.65) | copy-start | bytes 12292
  7.2 423.2 %reduce-scatter.4.cloned.1.call-start = ((), (), s32[]{:S(2)}) async-start(), calls=%async_computation.1 | async-start | bytes 786432
  8.2 24.4 %collective-permute-start = (bf16[2,2,16,8,128]{4,3,2,1,0:T(8,128)(2,1)S(1)}, bf16[2,2,16,8,128]{4,3,2,1,0:T(8,128)(2,1)S(1)}, u32[]{:S(2)}, u32[]{:S(2)}) collective-permute-start(bf16[2,2,16,8,128]{4,3,2,1,0:T(8,128)(2,1)S(1)} %slice.1486), channel_id=1, source_target_pairs={{0,2},{1,3},{4,6},{5,7},{8,10},{9,11},{12,14},{13,15},{16,18},{17,... | collective-permute-start | bytes 393224 | tf_op jit(solution)/shard_map/ppermute | solution.py:13
  35.0 2.3 copy-start.2
  45.6 2.2 copy-start.5
  55.7 1.8 copy-start.3
  229.8 31.2 %copy-start.6 = (bf16[1024,128]{1,0:T(8,128)(2,1)S(1)}, bf16[1024,128]{1,0:T(8,128)(2,1)}, u32[]{:S(2)}) copy-start(bf16[1024,128]{1,0:T(8,128)(2,1)} %copy-done.5) | copy-start | bytes 786436
  239.6 21.5 %collective-permute-start.1 = (f32[2,2,16,8,256]{4,3,2,1,0:T(8,128)S(1)}, f32[2,2,16,8,256]{4,3,2,1,0:T(8,128)S(1)}, u32[]{:S(2)}, u32[]{:S(2)}) collective-permute-start(f32[2,2,16,8,256]{4,3,2,1,0:T(8,128)S(1)} %slice.1599), channel_id=1, source_target_pairs={{2,0},{3,1},{6,4},{7,5},{10,8},{11,9},{14,12},{15,13},{18,16},{19,... | collective-permute-start | bytes 1572872 | tf_op jit(solution)/shard_map/ppermute | solution.py:13
  274.3 13.7 %copy-start.4 = (f32[27,256,128]{2,1,0:T(8,128)S(1)}, f32[27,256,128]{2,1,0:T(8,128)}, u32[]{:S(2)}) copy-start(f32[27,256,128]{2,1,0:T(8,128)} %copy-done.3) | copy-start | bytes 10616836
  288.0 155.3 %copy-start.1 = (bf16[128,16]{0,1:T(8,128)(2,1)S(1)}, bf16[128,16]{0,1:T(8,128)(2,1)}, u32[]{:S(2)}) copy-start(bf16[128,16]{0,1:T(8,128)(2,1)} %param.65) | copy-start | bytes 12292
Sparse Core Ops, SparseCore 0:
  288.1 10.2 reduce-scatter.3
where the time goes:
time: 454 us; the launch traced here: 450 us
  blocking collectives  177 us (39%)
  local copies, waits for them, and re-layouts  173 us (38%)
  matrix products  74.9 us (16%)
  between operations  14.6 us (3%)
  starting transfers between devices  6.18 us (1%)
    psum x1, blocking collectives, body(): lax.psum((grad_conv_local, grad_proj_local), ('cam', 'tm'))  142 us
    scatter-add x19, local copies, waits for them, and re-layouts, input_taps(): padded = padded.at[:, shift_t:shift_t + frames, shift_h:shift_h + height,...  125 us
    dot_general x27, matrix products, input_taps(): lax.dot_general(grad_rows, weight[tap_index], (((1,), (1,)), ((), ())), p...  55.4 us
    unnamed x20, local copies, waits for them, and re-layouts  40.4 us
    all_gather x1, blocking collectives, body(): block_in = lax.all_gather(cotangent, 'cam', axis=0, tiled=True)  13.6 us
    all_gather x1, blocking collectives, body(): block_in = lax.all_gather(latent_maps, 'cam', axis=0, tiled=True)  13.4 us
    dot_general x27, matrix products, weight_taps(): lax.dot_general(window, grad_rows, (((0,), (0,)), ((), ())), preferred_el...  9.49 us
  transfers between devices with their start and end apart: 3, of which 0 were waited for; matrix products, arithmetic and copies ran while one was open for 2% of the time, Pallas kernels for 0%

commit v1 on v0

--- a/solution.py
+++ b/solution.py
@@ -5,6 +5,11 @@
 
 KT = 3
 KS = 3
+
+
+def axis_by_axis(x, one, other):
+    half = lax.psum(x, one)
+    return lax.psum(half, other)
 
 
 def shifted(shard, axis, by):
@@ -135,7 +140,7 @@
     own_part = full_back[:, KT - 1 :]
     own_part = own_part.at[:, frames - (KT - 1) :].add(incoming)
     grad_conv_local = weight_taps(extended, dpre, frames, height, width)
-    grad_conv, grad_proj = lax.psum((grad_conv_local, grad_proj_local), ("cam", "tm"))
+    grad_conv, grad_proj = axis_by_axis((grad_conv_local, grad_proj_local), "tm", "cam")
     grad_video = lax.psum_scatter(
         own_part.astype(jnp.bfloat16), "chan", scatter_dimension=4, tiled=True
     )

time: 454 us -> 525 us (1.16)
  waiting for transfers between devices: 0.02 us -> 67.3 us
  matrix products: 74.9 us -> 85.4 us
  blocking collectives: 177 us -> 167 us
    psum x0 -> x1, waiting for transfers between devices: none -> 57.6 us  [axis_by_axis(): half = lax.psum(x, one)]
    psum x1 -> x2, blocking collectives: 142 us -> 132 us  [the longest x1 127 us: axis_by_axis(): return lax.psum(half, other)]
    ppermute x2, waiting for transfers between devices: 0.01 us -> 9.63 us  [shifted(): return lax.ppermute(shard, axis, pairs)]
    unnamed x20 -> x38, local copies, waits for them, and re-layouts: 40.4 us -> 40.3 us
  transfers between devices with their start and end apart: 3 -> 4, of which waited for: 0 -> 2; matrix products, arithmetic and copies ran while one was open for 2% -> 5% of each run, Pallas kernels for 0% -> 0%
where the time goes in v1:
time: 525 us; the launch traced here: 521 us
  local copies, waits for them, and re-layouts  175 us (33%)
  blocking collectives  167 us (32%)
  matrix products  85.4 us (16%)
  waiting for transfers between devices  67.3 us (13%)
  between operations  16.1 us (3%)
  starting transfers between devices  6.48 us (1%)
    psum x1, blocking collectives, axis_by_axis(): return lax.psum(half, other)  127 us
    scatter-add x19, local copies, waits for them, and re-layouts, input_taps(): padded = padded.at[:, shift_t:shift_t + frames, shift_h:shift_h + height,...  127 us
    dot_general x27, matrix products, input_taps(): lax.dot_general(grad_rows, weight[tap_index], (((1,), (1,)), ((), ())), p...  60.3 us
    psum x1, waiting for transfers between devices, axis_by_axis(): half = lax.psum(x, one)  57.6 us
    unnamed x38, local copies, waits for them, and re-layouts  40.3 us
    dot_general x27, matrix products, weight_taps(): lax.dot_general(window, grad_rows, (((0,), (0,)), ((), ())), preferred_el...  14.4 us
    all_gather x1, blocking collectives, body(): block_in = lax.all_gather(cotangent, 'cam', axis=0, tiled=True)  13.6 us
    all_gather x1, blocking collectives, body(): block_in = lax.all_gather(latent_maps, 'cam', axis=0, tiled=True)  13.4 us
  transfers between devices with their start and end apart: 4, of which 2 were waited for; matrix products, arithmetic and copies ran while one was open for 5% of the time, Pallas kernels for 0%

profile of v1, /device:TPU:0, one launch (start us, length us, event | category | flops | bytes accessed | tf_op | source)
XLA Modules:
  0.0 521.4 jit_solution(4568566891887017393)
XLA Ops:
  9.0 4.8 collective-permute-start
  16.2 13.6 %all_gather.15 = bf16[4,4,16,128]{3,2,1,0:T(8,128)(2,1)S(1)} all-gather(bf16[1,4,16,128]{3,2,1,0:T(8,128)(2,1)} %param.69), channel_id=1, replica_groups=mesh['groups'=2,'cam'=4,'tm'=2,'chan'=2] {'cam'}, dimensions={0}, use_global_device_ids=true | all-gather | bytes 81920 | tf_op jit(solution)/shard_map/all_gather | solution.py:119
  59.7 7.0 %scatter-add.95 = f32[2,6,18,10,256]{4,3,2,1,0:T(8,128)} dynamic-update-slice(f32[2,6,18,10,256]{4,3,2,1,0:T(8,128)} %scatter-add.94, f32[2,4,16,8,256]{4,3,2,1,0:T(8,128)} %convolution_add_fusion.25, s32[]{:T(128)} %constant.917.clone.1, s32[]{:T(128)} %constant.917.clone.1, s32[]{:T(128)} %constant.917.clone.1, s32[]{:T(128)} %constant.926.clone.1, s32[]{:T(128)} %constant.917.clone.1) | dynamic-update-slice | bytes 2097156 | tf_op jit(solution)/shard_map/scatter-add | solution.py:71
  69.5 7.0 %scatter-add.96 = f32[2,6,18,10,256]{4,3,2,1,0:T(8,128)} dynamic-update-slice(f32[2,6,18,10,256]{4,3,2,1,0:T(8,128)} %scatter-add.95, f32[2,4,16,8,256]{4,3,2,1,0:T(8,128)} %convolution_add_fusion.24, s32[]{:T(128)} %constant.917.clone.1, s32[]{:T(128)} %constant.917.clone.1, s32[]{:T(128)} %constant.917.clone.1, s32[]{:T(128)} %constant.924.clone.1, s32[]{:T(128)} %constant.917.clone.1) | dynamic-update-slice | bytes 2097156 | tf_op jit(solution)/shard_map/scatter-add | solution.py:71
  82.0 7.0 %scatter-add.100 = f32[2,6,18,10,256]{4,3,2,1,0:T(8,128)} dynamic-update-slice(f32[2,6,18,10,256]{4,3,2,1,0:T(8,128)} %fusion.7, f32[2,4,16,8,256]{4,3,2,1,0:T(8,128)} %convolution_add_fusion.22, s32[]{:T(128)} %constant.917.clone.1, s32[]{:T(128)} %constant.917.clone.1, s32[]{:T(128)} %constant.926.clone.1, s32[]{:T(128)} %constant.926.clone.1, s32[]{:T(128)} %constant.917.clone.1) | dynamic-update-slice | bytes 2097156 | tf_op jit(solution)/shard_map/scatter-add | solution.py:71
  89.1 4.8 convolution_add_fusion.21
  93.8 9.0 %scatter-add.101 = f32[2,6,18,10,256]{4,3,2,1,0:T(8,128)} dynamic-update-slice(f32[2,6,18,10,256]{4,3,2,1,0:T(8,128)} %scatter-add.100, f32[2,4,16,8,256]{4,3,2,1,0:T(8,128)} %convolution_add_fusion.21, s32[]{:T(128)} %constant.917.clone.1, s32[]{:T(128)} %bitcast.103, s32[]{:T(128)} %bitcast.104, s32[]{:T(128)} %bitcast.105, s32[]{:T(128)} %constant.917.clone.1) | dynamic-update-slice | bytes 2097156 | tf_op jit(solution)/shard_map/scatter-add | solution.py:71
  107.3 6.7 %scatter-add.105 = f32[2,6,18,10,256]{4,3,2,1,0:T(8,128)} dynamic-update-slice(f32[2,6,18,10,256]{4,3,2,1,0:T(8,128)} %fusion.6, f32[2,4,16,8,256]{4,3,2,1,0:T(8,128)S(1)} %convolution_add_fusion.19, s32[]{:T(128)} %constant.917.clone.1, s32[]{:T(128)} %constant.917.clone.1, s32[]{:T(128)} %constant.924.clone.1, s32[]{:T(128)} %constant.926.clone.1, s32[]{:T(128)} %constant.917.clone.1) | dynamic-update-slice | bytes 2097156 | tf_op jit(solution)/shard_map/scatter-add | solution.py:71
  115.9 6.7 %scatter-add.106 = f32[2,6,18,10,256]{4,3,2,1,0:T(8,128)} dynamic-update-slice(f32[2,6,18,10,256]{4,3,2,1,0:T(8,128)} %scatter-add.105, f32[2,4,16,8,256]{4,3,2,1,0:T(8,128)S(1)} %convolution_add_fusion.18, s32[]{:T(128)} %constant.917.clone.1, s32[]{:T(128)} %constant.917.clone.1, s32[]{:T(128)} %constant.924.clone.1, s32[]{:T(128)} %constant.924.clone.1, s32[]{:T(128)} %constant.917.clone.1) | dynamic-update-slice | bytes 2097156 | tf_op jit(solution)/shard_map/scatter-add | solution.py:71
  127.2 6.8 %scatter-add.110 = f32[2,6,18,10,256]{4,3,2,1,0:T(8,128)} dynamic-update-slice(f32[2,6,18,10,256]{4,3,2,1,0:T(8,128)} %fusion.5, f32[2,4,16,8,256]{4,3,2,1,0:T(8,128)S(1)} %convolution_add_fusion.16, s32[]{:T(128)} %constant.917.clone.1, s32[]{:T(128)} %constant.926.clone.1, s32[]{:T(128)} %constant.917.clone.1, s32[]{:T(128)} %constant.926.clone.1, s32[]{:T(128)} %constant.917.clone.1) | dynamic-update-slice | bytes 2097156 | tf_op jit(solution)/shard_map/scatter-add | solution.py:71
  135.9 6.8 %scatter-add.111 = f32[2,6,18,10,256]{4,3,2,1,0:T(8,128)} dynamic-update-slice(f32[2,6,18,10,256]{4,3,2,1,0:T(8,128)} %scatter-add.110, f32[2,4,16,8,256]{4,3,2,1,0:T(8,128)S(1)} %convolution_add_fusion.15, s32[]{:T(128)} %constant.917.clone.1, s32[]{:T(128)} %constant.926.clone.1, s32[]{:T(128)} %constant.917.clone.1, s32[]{:T(128)} %constant.924.clone.1, s32[]{:T(128)} %constant.917.clone.1) | dynamic-update-slice | bytes 2097156 | tf_op jit(solution)/shard_map/scatter-add | solution.py:71
  147.2 6.8 %scatter-add.115 = f32[2,6,18,10,256]{4,3,2,1,0:T(8,128)} dynamic-update-slice(f32[2,6,18,10,256]{4,3,2,1,0:T(8,128)} %fusion.4, f32[2,4,16,8,256]{4,3,2,1,0:T(8,128)S(1)} %convolution_add_fusion.13, s32[]{:T(128)} %constant.917.clone.1, s32[]{:T(128)} %constant.926.clone.1, s32[]{:T(128)} %constant.926.clone.1, s32[]{:T(128)} %constant.926.clone.1, s32[]{:T(128)} %constant.917.clone.1) | dynamic-update-slice | bytes 2097156 | tf_op jit(solution)/shard_map/scatter-add | solution.py:71
  155.9 6.8 %scatter-add.116 = f32[2,6,18,10,256]{4,3,2,1,0:T(8,128)} dynamic-update-slice(f32[2,6,18,10,256]{4,3,2,1,0:T(8,128)} %scatter-add.115, f32[2,4,16,8,256]{4,3,2,1,0:T(8,128)S(1)} %convolution_add_fusion.12, s32[]{:T(128)} %constant.917.clone.1, s32[]{:T(128)} %constant.926.clone.1, s32[]{:T(128)} %constant.926.clone.1, s32[]{:T(128)} %constant.924.clone.1, s32[]{:T(128)} %constant.917.clone.1) | dynamic-update-slice | bytes 2097156 | tf_op jit(solution)/shard_map/scatter-add | solution.py:71
  167.1 6.8 %scatter-add.120 = f32[2,6,18,10,256]{4,3,2,1,0:T(8,128)} dynamic-update-slice(f32[2,6,18,10,256]{4,3,2,1,0:T(8,128)} %fusion.3, f32[2,4,16,8,256]{4,3,2,1,0:T(8,128)S(1)} %convolution_add_fusion.10, s32[]{:T(128)} %constant.917.clone.1, s32[]{:T(128)} %constant.926.clone.1, s32[]{:T(128)} %constant.924.clone.1, s32[]{:T(128)} %constant.926.clone.1, s32[]{:T(128)} %constant.917.clone.1) | dynamic-update-slice | bytes 2097156 | tf_op jit(solution)/shard_map/scatter-add | solution.py:71
  175.8 6.8 %scatter-add.121 = f32[2,6,18,10,256]{4,3,2,1,0:T(8,128)} dynamic-update-slice(f32[2,6,18,10,256]{4,3,2,1,0:T(8,128)} %scatter-add.120, f32[2,4,16,8,256]{4,3,2,1,0:T(8,128)S(1)} %convolution_add_fusion.9, s32[]{:T(128)} %constant.917.clone.1, s32[]{:T(128)} %constant.926.clone.1, s32[]{:T(128)} %constant.924.clone.1, s32[]{:T(128)} %constant.924.clone.1, s32[]{:T(128)} %constant.917.clone.1) | dynamic-update-slice | bytes 2097156 | tf_op jit(solution)/shard_map/scatter-add | solution.py:71
  187.0 6.7 %scatter-add.125 = f32[2,6,18,10,256]{4,3,2,1,0:T(8,128)} dynamic-update-slice(f32[2,6,18,10,256]{4,3,2,1,0:T(8,128)} %fusion.2, f32[2,4,16,8,256]{4,3,2,1,0:T(8,128)S(1)} %convolution_add_fusion.7, s32[]{:T(128)} %constant.917.clone.1, s32[]{:T(128)} %constant.924.clone.1, s32[]{:T(128)} %constant.917.clone.1, s32[]{:T(128)} %constant.926.clone.1, s32[]{:T(128)} %constant.917.clone.1) | dynamic-update-slice | bytes 2097156 | tf_op jit(solution)/shard_map/scatter-add | solution.py:71
  195.6 6.7 %scatter-add.126 = f32[2,6,18,10,256]{4,3,2,1,0:T(8,128)} dynamic-update-slice(f32[2,6,18,10,256]{4,3,2,1,0:T(8,128)} %scatter-add.125, f32[2,4,16,8,256]{4,3,2,1,0:T(8,128)S(1)} %convolution_add_fusion.6, s32[]{:T(128)} %constant.917.clone.1, s32[]{:T(128)} %constant.924.clone.1, s32[]{:T(128)} %constant.917.clone.1, s32[]{:T(128)} %constant.924.clone.1, s32[]{:T(128)} %constant.917.clone.1) | dynamic-update-slice | bytes 2097156 | tf_op jit(solution)/shard_map/scatter-add | solution.py:71
  206.8 6.7 %scatter-add.130 = f32[2,6,18,10,256]{4,3,2,1,0:T(8,128)} dynamic-update-slice(f32[2,6,18,10,256]{4,3,2,1,0:T(8,128)} %fusion.1, f32[2,4,16,8,256]{4,3,2,1,0:T(8,128)S(1)} %convolution_add_fusion.4, s32[]{:T(128)} %constant.917.clone.1, s32[]{:T(128)} %constant.924.clone.1, s32[]{:T(128)} %constant.926.clone.1, s32[]{:T(128)} %constant.926.clone.1, s32[]{:T(128)} %constant.917.clone.1) | dynamic-update-slice | bytes 2097156 | tf_op jit(solution)/shard_map/scatter-add | solution.py:71
  215.3 6.7 %scatter-add.131 = f32[2,6,18,10,256]{4,3,2,1,0:T(8,128)} dynamic-update-slice(f32[2,6,18,10,256]{4,3,2,1,0:T(8,128)} %scatter-add.130, f32[2,4,16,8,256]{4,3,2,1,0:T(8,128)S(1)} %convolution_add_fusion.3, s32[]{:T(128)} %constant.917.clone.1, s32[]{:T(128)} %constant.924.clone.1, s32[]{:T(128)} %constant.926.clone.1, s32[]{:T(128)} %constant.924.clone.1, s32[]{:T(128)} %constant.917.clone.1) | dynamic-update-slice | bytes 2097156 | tf_op jit(solution)/shard_map/scatter-add | solution.py:71
  226.5 6.8 %scatter-add.135 = f32[2,6,18,10,256]{4,3,2,1,0:T(8,128)} dynamic-update-slice(f32[2,6,18,10,256]{4,3,2,1,0:T(8,128)} %fusion, f32[2,4,16,8,256]{4,3,2,1,0:T(8,128)S(1)} %convolution_add_fusion.1, s32[]{:T(128)} %constant.917.clone.1, s32[]{:T(128)} %constant.924.clone.1, s32[]{:T(128)} %constant.924.clone.1, s32[]{:T(128)} %constant.926.clone.1, s32[]{:T(128)} %constant.917.clone.1) | dynamic-update-slice | bytes 2097156 | tf_op jit(solution)/shard_map/scatter-add | solution.py:71
  233.3 2.9 convolution_add_fusion
  236.2 7.1 %scatter-add.136 = f32[2,6,18,10,256]{4,3,2,1,0:T(8,128)} dynamic-update-slice(f32[2,6,18,10,256]{4,3,2,1,0:T(8,128)} %scatter-add.135, f32[2,4,16,8,256]{4,3,2,1,0:T(8,128)} %convolution_add_fusion, s32[]{:T(128)} %constant.917.clone.1, s32[]{:T(128)} %constant.924.clone.1, s32[]{:T(128)} %constant.924.clone.1, s32[]{:T(128)} %constant.924.clone.1, s32[]{:T(128)} %constant.917.clone.1) | dynamic-update-slice | bytes 2097156 | tf_op jit(solution)/shard_map/scatter-add | solution.py:71
  250.8 9.6 %collective-permute-done.1 = f32[2,2,16,8,256]{4,3,2,1,0:T(8,128)S(1)} collective-permute-done((f32[2,2,16,8,256]{4,3,2,1,0:T(8,128)S(1)}, f32[2,2,16,8,256]{4,3,2,1,0:T(8,128)S(1)}, u32[]{:S(2)}, u32[]{:S(2)}) %collective-permute-start.1) | collective-permute-done | bytes 524320 | tf_op jit(solution)/shard_map/ppermute | solution.py:18
  261.7 11.8 %copy.48 = bf16[2,4,16,8,256]{3,2,1,0,4:T(8,128)(2,1)} copy(bf16[2,4,16,8,256]{4,3,2,1,0:T(8,128)(2,1)S(1)} %fusion.37) | data formatting | bytes 1048576
  273.5 13.6 %reshape.1527 = bf16[256,1024]{1,0:T(8,128)(2,1)} reshape(bf16[256,2,4,16,8]{4,3,2,1,0:T(8,128)(2,1)} %bitcast.557) | data formatting | bytes 1048576
  292.4 3.6 psum.35
  296.4 13.4 %all_gather.14 = bf16[8,4,16,128]{3,2,1,0:T(8,128)(2,1)S(1)} all-gather(bf16[2,4,16,128]{3,2,1,0:T(8,128)(2,1)S(1)} %reshape.1490), channel_id=1, replica_groups=mesh['groups'=2,'cam'=4,'tm'=2,'chan'=2] {'cam'}, dimensions={0}, use_global_device_ids=true | all-gather | bytes 163840 | tf_op jit(solution)/shard_map/all_gather | solution.py:109
  310.0 5.1 psum.38
  316.0 6.8 %reshape.1528 = bf16[128,2,4,16,8]{4,3,2,1,0:T(8,128)(2,1)} reshape(bf16[128,1024]{1,0:T(8,128)(2,1)} %reduce-scatter.4.cloned.1.call-done) | data formatting | bytes 524288
  322.9 6.1 %copy.49 = bf16[2,4,16,8,128]{4,3,2,1,0:T(8,128)(2,1)} copy(bf16[2,4,16,8,128]{3,2,1,0,4:T(8,128)(2,1)} %bitcast.558) | data formatting | bytes 524288
  329.0 57.6 %all-reduce.6.cloned.1.call-done = f32[27,256,128]{2,1,0:T(8,128)} async-done(((f32[27,256,128]{2,1,0:T(8,128)}), f32[27,256,128]{2,1,0:T(8,128)}) %all-reduce.6.cloned.1.call-update) | async-done | bytes 3538960 | tf_op jit(solution)/shard_map/psum | solution.py:11
  386.6 127.3 %all-reduce.7 = (bf16[27,256,128]{2,1,0:T(8,128)(2,1)}, f32[128,16]{0,1:T(8,128)}) all-reduce(f32[27,256,128]{2,1,0:T(8,128)} %all-reduce.6.cloned.1.call-done, f32[128,16]{0,1:T(8,128)S(1)} %psum.38), channel_id=1, replica_groups=mesh['groups'=2,'cam'=4,'tm'=2,'chan'=2] {'cam'}, use_global_device_ids=true, to_apply=%region_6.7 | all-reduce | flops 886784 | bytes 5324800 | tf_op jit(solution)/shard_map/psum | solution.py:12
  (145 shorter events, 99.4 us)
Async XLA Ops:
  8.0 39.2 %copy-start = (bf16[128,16]{0,1:T(8,128)(2,1)S(1)}, bf16[128,16]{0,1:T(8,128)(2,1)}, u32[]{:S(2)}) copy-start(bf16[128,16]{0,1:T(8,128)(2,1)} %param.65) | copy-start | bytes 12292
  8.0 308.0 %reduce-scatter.4.cloned.1.call-start = ((), (), s32[]{:S(2)}) async-start(), calls=%async_computation.2 | async-start | bytes 786432
  9.0 24.4 %collective-permute-start = (bf16[2,2,16,8,128]{4,3,2,1,0:T(8,128)(2,1)S(1)}, bf16[2,2,16,8,128]{4,3,2,1,0:T(8,128)(2,1)S(1)}, u32[]{:S(2)}, u32[]{:S(2)}) collective-permute-start(bf16[2,2,16,8,128]{4,3,2,1,0:T(8,128)(2,1)S(1)} %slice.1486), channel_id=1, source_target_pairs={{0,2},{1,3},{4,6},{5,7},{8,10},{9,11},{12,14},{13,15},{16,18},{17,... | collective-permute-start | bytes 393224 | tf_op jit(solution)/shard_map/ppermute | solution.py:18
  35.9 8.7 %copy-start.6 = (bf16[2,4,16,8,256]{4,3,2,1,0:T(8,128)(2,1)}, bf16[2,4,16,8,256]{4,3,2,1,0:T(8,128)(2,1)S(1)}, u32[]{:S(2)}) copy-start(bf16[2,4,16,8,256]{4,3,2,1,0:T(8,128)(2,1)S(1)} %get-tuple-element.364) | copy-start | bytes 1572868
  35.9 9.4 %copy-start.4 = (bf16[2,4,16,8,256]{4,3,2,1,0:T(8,128)(2,1)}, bf16[2,4,16,8,256]{4,3,2,1,0:T(8,128)(2,1)S(1)}, u32[]{:S(2)}) copy-start(bf16[2,4,16,8,256]{4,3,2,1,0:T(8,128)(2,1)S(1)} %get-tuple-element.365) | copy-start | bytes 1572868
  35.9 9.7 %copy-start.2 = (bf16[2,4,16,8,256]{4,3,2,1,0:T(8,128)(2,1)}, bf16[2,4,16,8,256]{4,3,2,1,0:T(8,128)(2,1)S(1)}, u32[]{:S(2)}) copy-start(bf16[2,4,16,8,256]{4,3,2,1,0:T(8,128)(2,1)S(1)} %get-tuple-element.366) | copy-start | bytes 1572868
  35.9 2.3 copy-start.1
  38.2 5.8 %copy-start.10 = (bf16[2,4,16,8,256]{4,3,2,1,0:T(8,128)(2,1)}, bf16[2,4,16,8,256]{4,3,2,1,0:T(8,128)(2,1)S(1)}, u32[]{:S(2)}) copy-start(bf16[2,4,16,8,256]{4,3,2,1,0:T(8,128)(2,1)S(1)} %get-tuple-element.361) | copy-start | bytes 1572868
  38.2 6.1 %copy-start.8 = (bf16[2,4,16,8,256]{4,3,2,1,0:T(8,128)(2,1)}, bf16[2,4,16,8,256]{4,3,2,1,0:T(8,128)(2,1)S(1)}, u32[]{:S(2)}) copy-start(bf16[2,4,16,8,256]{4,3,2,1,0:T(8,128)(2,1)S(1)} %get-tuple-element.362) | copy-start | bytes 1572868
  38.2 7.9 %copy-start.13 = (bf16[2,4,16,8,256]{4,3,2,1,0:T(8,128)(2,1)}, bf16[2,4,16,8,256]{4,3,2,1,0:T(8,128)(2,1)S(1)}, u32[]{:S(2)}) copy-start(bf16[2,4,16,8,256]{4,3,2,1,0:T(8,128)(2,1)S(1)} %get-tuple-element.344) | copy-start | bytes 1572868
  54.1 1.8 copy-start.12
  226.5 19.6 %copy-start.11 = (bf16[2,4,16,8,256]{4,3,2,1,0:T(8,128)(2,1)S(1)}, bf16[2,4,16,8,256]{4,3,2,1,0:T(8,128)(2,1)}, u32[]{:S(2)}) copy-start(bf16[2,4,16,8,256]{4,3,2,1,0:T(8,128)(2,1)} %copy-done.10) | copy-start | bytes 1572868
  233.2 15.5 %copy-start.9 = (bf16[2,4,16,8,256]{4,3,2,1,0:T(8,128)(2,1)S(1)}, bf16[2,4,16,8,256]{4,3,2,1,0:T(8,128)(2,1)}, u32[]{:S(2)}) copy-start(bf16[2,4,16,8,256]{4,3,2,1,0:T(8,128)(2,1)} %copy-done.8) | copy-start | bytes 1572868
  236.2 13.6 %copy-start.7 = (bf16[2,4,16,8,256]{4,3,2,1,0:T(8,128)(2,1)S(1)}, bf16[2,4,16,8,256]{4,3,2,1,0:T(8,128)(2,1)}, u32[]{:S(2)}) copy-start(bf16[2,4,16,8,256]{4,3,2,1,0:T(8,128)(2,1)} %copy-done.6) | copy-start | bytes 1572868
  244.5 15.9 %collective-permute-start.1 = (f32[2,2,16,8,256]{4,3,2,1,0:T(8,128)S(1)}, f32[2,2,16,8,256]{4,3,2,1,0:T(8,128)S(1)}, u32[]{:S(2)}, u32[]{:S(2)}) collective-permute-start(f32[2,2,16,8,256]{4,3,2,1,0:T(8,128)S(1)} %slice.1599), channel_id=1, source_target_pairs={{2,0},{3,1},{6,4},{7,5},{10,8},{11,9},{14,12},{15,13},{18,16},{19,... | collective-permute-start | bytes 1572872 | tf_op jit(solution)/shard_map/ppermute | solution.py:18
  273.5 14.7 %copy-start.5 = (bf16[2,4,16,8,256]{4,3,2,1,0:T(8,128)(2,1)S(1)}, bf16[2,4,16,8,256]{4,3,2,1,0:T(8,128)(2,1)}, u32[]{:S(2)}) copy-start(bf16[2,4,16,8,256]{4,3,2,1,0:T(8,128)(2,1)} %copy-done.4) | copy-start | bytes 1572868
  273.5 15.6 %copy-start.3 = (bf16[2,4,16,8,256]{4,3,2,1,0:T(8,128)(2,1)S(1)}, bf16[2,4,16,8,256]{4,3,2,1,0:T(8,128)(2,1)}, u32[]{:S(2)}) copy-start(bf16[2,4,16,8,256]{4,3,2,1,0:T(8,128)(2,1)} %copy-done.2) | copy-start | bytes 1572868
  287.1 4.0 copy-start.14
  287.1 99.5 %all-reduce.6.cloned.1.call-start = ((), (), s32[]{:S(2)}) async-start(), calls=%async_computation.1 | async-start | bytes 7077888 | tf_op jit(solution)/shard_map/psum | solution.py:11
  288.2 4.0 copy-start.15
Sparse Core Ops, SparseCore 0:
  287.3 8.0 reduce-scatter.3
Sparse Core Ops, SparseCore 1:
  292.3 94.3 all-reduce.5
